TPU v7x, 128 devices: a whole 4x4x4 slice. The times are simulated.
128 devices in a mesh: gx: 8 (over x, core), yz: 16 (over z, y).
Axes of the slice: x: 4, y: 4, z: 4, core: 2. Of those that a mesh axis runs over, the one named last changes fastest.
Arguments:
- hidden_in: bfloat16 [2, 128, 8192], P(None, ('gx', 'yz')), may hold values from -6 to 6
- k_cache: bfloat16 [128, 1024, 1024], P(('gx', 'yz'))
- v_cache: bfloat16 [128, 1024, 1024], P(('gx', 'yz')), may hold values from -6 to 6
- lengths: int32 [128], P(('gx', 'yz')), may hold values from 1 to 1024, as said below
- counts: int32 [128, 16], P(('gx', 'yz')), may hold values from 0 to 3
- token_elem: int32 [512], replicated, may hold values from 0 to 16, as said below
- tokens: int32 [128], P(('gx', 'yz')), may hold values from 0 to 511
- attn_gain: float32 [8192], replicated, may hold values from 0.5 to 1.5
- qkv_weight: bfloat16 [8192, 10240], P('gx', 'yz'), may hold values from -0.0625 to 0.0625
- o_weight: bfloat16 [8192, 8192], P('gx', 'yz'), may hold values from -0.0625 to 0.0625
- ffn_gain: float32 [8192], replicated, may hold values from 0.5 to 1.5
- gate_up_weight: bfloat16 [8192, 57344], P('gx', 'yz'), may hold values from -0.0625 to 0.0625
- down_weight: bfloat16 [28672, 8192], P('gx', 'yz'), may hold values from -0.03125 to 0.03125
- final_gain: float32 [8192], replicated, may hold values from 0.5 to 1.5
- lm_weight: bfloat16 [8192, 512], P(('gx', 'yz'))
Outputs:
- layer_out: bfloat16 [2, 128, 8192], P(None, ('gx', 'yz'))
- log_probs: float32 [2, 128, 512], P(None, ('gx', 'yz'))
Inputs may be any that keep to these rules, and one draw needn't show every extreme that they name: `lengths`: some spectrum uses all 1024 positions. `token_elem`: some token has no element (value 16).
All inputs are finite; a program needn't handle non-finite values.
Results may differ from a plain program's by a relative error of at most 0.022.
Values may be sent and summed in bfloat16 or wider, within the bound.
No kernel may reach another device: no remote copies, remote signals or barrier semaphores. Data moves between devices by JAX's collectives and lax.ppermute only.
A program may use at most 128 MiB of HBM per device.

v0:
```python
import math
import jax
import jax.numpy as jnp
from jax import lax
from jax.sharding import PartitionSpec as P

FF = 28672
HEADS = 64
KV_HEADS = 8
HEAD = 128
VOCAB = 512
ELEMENTS = 16
NORM_EPS = 1e-05
ROPE_THETA = 500000.0


def norm_rows(values, gain_vec):
    wide = values.astype(jnp.float32)
    inverse = lax.rsqrt(jnp.mean(wide * wide, axis=-1, keepdims=True) + NORM_EPS)
    return (wide * inverse * gain_vec).astype(jnp.bfloat16)


def rotate(heads_in, positions):
    half_width = heads_in.shape[-1] // 2
    frequency = jnp.power(
        ROPE_THETA, -(jnp.arange(half_width, dtype=jnp.float32) * 2.0 / heads_in.shape[-1])
    )
    angles = positions.astype(jnp.float32)[:, None] * frequency[None, :]
    cos_part = jnp.cos(angles)[:, None, :]
    sin_part = jnp.sin(angles)[:, None, :]
    wide = heads_in.astype(jnp.float32)
    first_half = wide[..., :half_width]
    second_half = wide[..., half_width:]
    joined = jnp.concatenate(
        [
            first_half * cos_part - second_half * sin_part,
            second_half * cos_part + first_half * sin_part,
        ],
        -1,
    )
    return joined.astype(jnp.bfloat16)


def spread_rows(inputs):
    gathered = lax.all_gather(inputs, "yz", axis=0, tiled=True)
    return lax.all_to_all(gathered, "gx", split_axis=1, concat_axis=0, tiled=True)


def project(inputs, weight):
    spread = spread_rows(inputs)
    summed = lax.psum_scatter(
        jnp.dot(spread, weight, preferred_element_type=jnp.float32),
        "gx",
        scatter_dimension=0,
        tiled=True,
    )
    return lax.all_to_all(
        summed.astype(jnp.bfloat16), "yz", split_axis=0, concat_axis=1, tiled=True
    )


def head_logits(normed, lm_weight):
    slice_width = lm_weight.shape[0]
    offset_cols = lax.axis_index("yz") * slice_width
    spread = spread_rows(normed)
    own_cols = lax.dynamic_slice_in_dim(spread, offset_cols, slice_width, 1)
    return lax.psum_scatter(
        jnp.dot(own_cols, lm_weight, preferred_element_type=jnp.float32),
        ("gx", "yz"),
        scatter_dimension=0,
        tiled=True,
    )


def attend(queries, k_cache, v_cache, lengths, keys_new, values_new):
    groups = HEADS // KV_HEADS
    factor = 1.0 / math.sqrt(HEAD)
    rows_here = queries.shape[0]
    cache_len = k_cache.shape[1]
    fresh = keys_new.shape[1]
    query_heads = queries.reshape(rows_here, KV_HEADS, groups, HEAD)
    kcache_heads = k_cache.reshape(rows_here, cache_len, KV_HEADS, HEAD)
    vcache_heads = v_cache.reshape(rows_here, cache_len, KV_HEADS, HEAD)
    knew_heads = keys_new.reshape(rows_here, fresh, KV_HEADS, HEAD)
    vnew_heads = values_new.reshape(rows_here, fresh, KV_HEADS, HEAD)
    scores_cache = (
        jnp.einsum("rkgd,rlkd->rkgl", query_heads, kcache_heads, preferred_element_type=jnp.float32)
        * factor
    )
    valid = jnp.arange(cache_len)[None, None, None, :] < lengths[:, None, None, None]
    scores_cache = jnp.where(valid, scores_cache, -jnp.inf)
    scores_new = (
        jnp.einsum("rkgd,rnkd->rkgn", query_heads, knew_heads, preferred_element_type=jnp.float32)
        * factor
    )
    largest = jnp.maximum(jnp.max(scores_cache, -1), jnp.max(scores_new, -1))[..., None]
    exp_cache = jnp.where(valid, jnp.exp(scores_cache - largest), 0.0)
    exp_new = jnp.exp(scores_new - largest)
    denominator = jnp.sum(exp_cache, -1, keepdims=True) + jnp.sum(exp_new, -1, keepdims=True)
    weights_cache = (exp_cache / denominator).astype(jnp.bfloat16)
    weights_new = (exp_new / denominator).astype(jnp.bfloat16)
    result = jnp.einsum(
        "rkgl,rlkd->rkgd", weights_cache, vcache_heads, preferred_element_type=jnp.float32
    )
    result = result + jnp.einsum(
        "rkgn,rnkd->rkgd", weights_new, vnew_heads, preferred_element_type=jnp.float32
    )
    return result.reshape(rows_here, HEADS * HEAD).astype(jnp.bfloat16)


def element_table(token_elem):
    return (token_elem[:, None] == jnp.arange(ELEMENTS, dtype=jnp.int32)[None, :]).astype(
        jnp.float32
    )


def masked_log_probs(logits, remaining, token_elem):
    element_hot = element_table(token_elem)
    per_token = jnp.dot(remaining, element_hot.T)
    allowed = (per_token > 0.5) | (token_elem == ELEMENTS)[None, :]
    largest = jnp.max(jnp.where(allowed, logits, -jnp.inf), -1, keepdims=True)
    shifted = logits - largest
    denominator = jnp.sum(jnp.where(allowed, jnp.exp(shifted), 0.0), -1, keepdims=True)
    return jnp.where(allowed, shifted - jnp.log(denominator), 0.0)


def used_elements(tokens, token_elem):
    token_hot = (tokens[:, None] == jnp.arange(VOCAB, dtype=jnp.int32)[None, :]).astype(jnp.float32)
    return jnp.dot(token_hot, element_table(token_elem))


def per_device(
    hidden_in,
    k_cache,
    v_cache,
    lengths,
    counts,
    token_elem,
    tokens,
    attn_gain,
    qkv_weight,
    o_weight,
    ffn_gain,
    gate_up_weight,
    down_weight,
    final_gain,
    lm_weight,
):
    q_width = HEADS * HEAD
    kv_width = KV_HEADS * HEAD
    key_list = []
    value_list = []
    result_list = []
    logit_steps = []
    for which_step in range(2):
        positions = lengths + which_step
        mixed = project(norm_rows(hidden_in[which_step], attn_gain), qkv_weight)
        queries = rotate(mixed[:, :q_width].reshape(-1, HEADS, HEAD), positions).reshape(
            -1, q_width
        )
        keys_now = rotate(
            mixed[:, q_width : q_width + kv_width].reshape(-1, KV_HEADS, HEAD), positions
        ).reshape(-1, kv_width)
        queries, keys_now, values_now = (queries, keys_now, mixed[:, q_width + kv_width :])
        key_list.append(keys_now)
        value_list.append(values_now)
        attended = attend(
            queries, k_cache, v_cache, lengths, jnp.stack(key_list, 1), jnp.stack(value_list, 1)
        )
        projected = project(attended, o_weight)
        residual = (
            hidden_in[which_step].astype(jnp.float32) + projected.astype(jnp.float32)
        ).astype(jnp.bfloat16)
        gate_up = project(norm_rows(residual, ffn_gain), gate_up_weight)
        hidden_units = (
            jax.nn.silu(gate_up[:, :FF].astype(jnp.float32)) * gate_up[:, FF:].astype(jnp.float32)
        ).astype(jnp.bfloat16)
        lowered = project(hidden_units, down_weight)
        result = (residual.astype(jnp.float32) + lowered.astype(jnp.float32)).astype(jnp.bfloat16)
        logits = head_logits(norm_rows(result, final_gain), lm_weight)
        result, logits = (result, logits)
        result_list.append(result)
        logit_steps.append(logits)
    outputs = jnp.stack(result_list)
    remaining = counts.astype(jnp.float32)
    first_log = masked_log_probs(logit_steps[0], remaining, token_elem)
    remaining = remaining - used_elements(tokens, token_elem)
    second_log = masked_log_probs(logit_steps[1], remaining, token_elem)
    return (outputs, jnp.stack([first_log, second_log]))


def solution(mesh):
    return jax.shard_map(
        per_device,
        mesh=mesh,
        in_specs=(
            P(None, ("gx", "yz"), None),
            P(("gx", "yz"), None, None),
            P(("gx", "yz"), None, None),
            P(("gx", "yz")),
            P(("gx", "yz"), None),
            P(),
            P(("gx", "yz")),
            P(),
            P("gx", "yz"),
            P("gx", "yz"),
            P(),
            P("gx", "yz"),
            P("gx", "yz"),
            P(),
            P(("gx", "yz"), None),
        ),
        out_specs=(P(None, ("gx", "yz"), None), P(None, ("gx", "yz"), None)),
        check_vma=False,
    )
```

profile of v0, /device:TPU:1, one launch (start us, length us, event | category | flops | bytes accessed | tf_op | source)
XLA Modules:
  0.0 964.6 jit_solution(5913646445156775769)
XLA Ops:
  8.2 1.4 fusion.59
  11.1 20.9 %all-gather = bf16[131072]{0:T(1024)(128)(2,1)S(1)} all-gather(bf16[8192]{0:T(1024)(128)(2,1)S(1)} %multiply_convert_fusion.3), channel_id=2, replica_groups=mesh['gx'=8,'yz'=16] {'yz'}, dimensions={0}, use_global_device_ids=true | all-gather | bytes 278528 | tf_op jit(solution)/shard_map/all_gather | solution.py:45
  32.2 16.4 %all_to_all.306 = bf16[16,8,1024]{2,0,1:T(8,128)(2,1)S(1)} all-to-all(bf16[16,8,1024]{2,0,1:T(8,128)(2,1)S(1)} %copy.63), channel_id=1, replica_groups=mesh['gx'=8,'yz'=16] {'gx'}, dimensions={1} | all-to-all | bytes 524288 | tf_op jit(solution)/shard_map/all_to_all | solution.py:46
  50.5 25.7 %reduce-scatter.9.cloned.1.call-done = f32[16,640]{1,0:T(8,128)} async-done(((f32[128,640]{1,0:T(8,128)}), f32[16,640]{1,0:T(8,128)}) %reduce-scatter.9.cloned.1.call-update) | async-done | bytes 40976 | tf_op jit(solution)/shard_map/reduce_scatter | solution.py:51
  78.7 6.8 all-to-all-start.1
  85.5 2.4 copy.97
  87.9 2.0 copy.98
  89.9 2.0 all-to-all-done.1
  94.9 18.7 %all-gather.6 = bf16[16,1,8192]{2,1,0:T(2,128)(2,1)} all-gather(bf16[1,1,8192]{2,1,0:T(2,128)(2,1)S(1)} %reshape.875), channel_id=1, replica_groups=mesh['gx'=8,'yz'=16] {'yz'}, dimensions={0}, use_global_device_ids=true | all-gather | bytes 278528 | tf_op jit(solution)/shard_map/all_gather | solution.py:45
  113.7 3.3 reduce.22
  117.9 18.7 %all_to_all.307 = bf16[16,8,1024]{2,0,1:T(8,128)(2,1)S(1)} all-to-all(bf16[16,8,1024]{2,0,1:T(8,128)(2,1)S(1)} %bitcast.213), channel_id=1, replica_groups=mesh['gx'=8,'yz'=16] {'gx'}, dimensions={1} | all-to-all | bytes 524288 | tf_op jit(solution)/shard_map/all_to_all | solution.py:46
  136.6 2.3 fusion.104
  138.9 25.7 %reduce-scatter.11.cloned.1.call-done = f32[16,512]{1,0:T(8,128)} async-done(((f32[128,512]{1,0:T(8,128)}), f32[16,512]{1,0:T(8,128)}) %reduce-scatter.11.cloned.1.call-update) | async-done | bytes 32784 | tf_op jit(solution)/shard_map/reduce_scatter | solution.py:51
  166.0 13.0 %all_to_all.308 = bf16[16,2,256]{2,1,0:T(2,128)(2,1)S(1)} all-to-all(bf16[16,2,256]{2,1,0:T(2,128)(2,1)S(1)} %reshape.903), channel_id=1, replica_groups=mesh['gx'=8,'yz'=16] {'yz'}, dimensions={0} | all-to-all | bytes 32768 | tf_op jit(solution)/shard_map/all_to_all | solution.py:57
  183.2 18.3 %all-gather.1 = bf16[131072]{0:T(1024)(128)(2,1)} all-gather(bf16[8192]{0:T(1024)(128)(2,1)S(1)} %get-tuple-element.10), channel_id=3, replica_groups=mesh['gx'=8,'yz'=16] {'yz'}, dimensions={0}, use_global_device_ids=true | all-gather | bytes 278528 | tf_op jit(solution)/shard_map/all_gather | solution.py:45
  201.4 1.8 all_to_all.241
  204.3 18.9 %all_to_all.309 = bf16[16,8,1024]{2,0,1:T(8,128)(2,1)S(1)} all-to-all(bf16[16,8,1024]{2,0,1:T(8,128)(2,1)S(1)} %copy.70), channel_id=1, replica_groups=mesh['gx'=8,'yz'=16] {'gx'}, dimensions={1} | all-to-all | bytes 524288 | tf_op jit(solution)/shard_map/all_to_all | solution.py:46
  223.2 5.5 fusion.105
  228.7 27.9 %reduce-scatter.13.cloned.1.call-done = f32[16,3584]{1,0:T(8,128)} async-done(((f32[128,3584]{1,0:T(8,128)}), f32[16,3584]{1,0:T(8,128)}) %reduce-scatter.13.cloned.1.call-update) | async-done | bytes 229392 | tf_op jit(solution)/shard_map/reduce_scatter | solution.py:51
  256.6 1.6 convert_bitcast_fusion.3
  258.2 2.1 reduce.28
  260.3 1.6 reshape.905
  261.9 13.7 %all_to_all.310 = bf16[16,2,1792]{2,1,0:T(2,128)(2,1)} all-to-all(bf16[16,2,1792]{2,1,0:T(2,128)(2,1)} %reshape.905), channel_id=1, replica_groups=mesh['gx'=8,'yz'=16] {'yz'}, dimensions={0} | all-to-all | bytes 229376 | tf_op jit(solution)/shard_map/all_to_all | solution.py:57
  275.6 1.7 reshape.906
  278.5 21.8 %all-gather.7 = bf16[16,1,28672]{2,1,0:T(2,128)(2,1)} all-gather(bf16[1,1,28672]{2,1,0:T(2,128)(2,1)S(1)} %convert_bitcast_fusion.2), channel_id=1, replica_groups=mesh['gx'=8,'yz'=16] {'yz'}, dimensions={0}, use_global_device_ids=true | all-gather | bytes 974848 | tf_op jit(solution)/shard_map/all_gather | solution.py:45
  300.3 7.8 reduce.23
  309.5 25.2 %all_to_all.311 = bf16[16,8,3584]{2,0,1:T(8,128)(2,1)S(1)} all-to-all(bf16[16,8,3584]{2,0,1:T(8,128)(2,1)S(1)} %bitcast.204), channel_id=1, replica_groups=mesh['gx'=8,'yz'=16] {'gx'}, dimensions={1} | all-to-all | bytes 1835008 | tf_op jit(solution)/shard_map/all_to_all | solution.py:46
  336.2 25.6 %reduce-scatter.15.cloned.1.call-done = f32[16,512]{1,0:T(8,128)} async-done(((f32[128,512]{1,0:T(8,128)}), f32[16,512]{1,0:T(8,128)}) %reduce-scatter.15.cloned.1.call-update) | async-done | bytes 32784 | tf_op jit(solution)/shard_map/reduce_scatter | solution.py:51
  363.1 13.0 %all_to_all.312 = bf16[16,2,256]{2,1,0:T(2,128)(2,1)S(1)} all-to-all(bf16[16,2,256]{2,1,0:T(2,128)(2,1)S(1)} %reshape.907), channel_id=1, replica_groups=mesh['gx'=8,'yz'=16] {'yz'}, dimensions={0} | all-to-all | bytes 32768 | tf_op jit(solution)/shard_map/all_to_all | solution.py:57
  379.8 18.3 %all-gather.2 = bf16[131072]{0:T(1024)(128)(2,1)} all-gather(bf16[8192]{0:T(1024)(128)(2,1)S(1)} %multiply_convert_fusion.2), channel_id=4, replica_groups=mesh['gx'=8,'yz'=16] {'yz'}, dimensions={0}, use_global_device_ids=true | all-gather | bytes 278528 | tf_op jit(solution)/shard_map/all_gather | solution.py:45
  398.1 1.8 all_to_all.254
  400.9 18.9 %all_to_all.313 = bf16[16,8,1024]{2,0,1:T(8,128)(2,1)S(1)} all-to-all(bf16[16,8,1024]{2,0,1:T(8,128)(2,1)S(1)} %copy.75), channel_id=1, replica_groups=mesh['gx'=8,'yz'=16] {'gx'}, dimensions={1} | all-to-all | bytes 524288 | tf_op jit(solution)/shard_map/all_to_all | solution.py:46
  421.6 25.1 %reduce-scatter.17.cloned.1.call-done = f32[16,640]{1,0:T(8,128)} async-done(((f32[128,640]{1,0:T(8,128)}), f32[16,640]{1,0:T(8,128)}) %reduce-scatter.17.cloned.1.call-update) | async-done | bytes 40976 | tf_op jit(solution)/shard_map/reduce_scatter | solution.py:51
  448.1 1.9 reduce.30
  451.4 6.9 all-to-all-start.9
  459.0 5.8 all-to-all-done.9
  464.8 1.5 reshape.910
  471.5 16.9 %all-gather.8 = bf16[16,1,8192]{2,1,0:T(2,128)(2,1)S(1)} all-gather(bf16[1,1,8192]{2,1,0:T(2,128)(2,1)S(1)} %reshape.879), channel_id=1, replica_groups=mesh['gx'=8,'yz'=16] {'yz'}, dimensions={0}, use_global_device_ids=true | all-gather | bytes 278528 | tf_op jit(solution)/shard_map/all_gather | solution.py:45
  488.5 1.5 reduce.24
  490.1 18.7 %all_to_all.314 = bf16[16,8,1024]{2,0,1:T(8,128)(2,1)S(1)} all-to-all(bf16[16,8,1024]{2,0,1:T(8,128)(2,1)S(1)} %bitcast.214), channel_id=1, replica_groups=mesh['gx'=8,'yz'=16] {'gx'}, dimensions={1} | all-to-all | bytes 524288 | tf_op jit(solution)/shard_map/all_to_all | solution.py:46
  509.9 25.7 %reduce-scatter.19.cloned.1.call-done = f32[16,512]{1,0:T(8,128)} async-done(((f32[128,512]{1,0:T(8,128)}), f32[16,512]{1,0:T(8,128)}) %reduce-scatter.19.cloned.1.call-update) | async-done | bytes 32784 | tf_op jit(solution)/shard_map/reduce_scatter | solution.py:51
  536.9 13.0 %all_to_all.315 = bf16[16,2,256]{2,1,0:T(2,128)(2,1)S(1)} all-to-all(bf16[16,2,256]{2,1,0:T(2,128)(2,1)S(1)} %reshape.911), channel_id=1, replica_groups=mesh['gx'=8,'yz'=16] {'yz'}, dimensions={0} | all-to-all | bytes 32768 | tf_op jit(solution)/shard_map/all_to_all | solution.py:57
  551.4 16.7 %all-gather.3 = bf16[131072]{0:T(1024)(128)(2,1)S(1)} all-gather(bf16[8192]{0:T(1024)(128)(2,1)S(1)} %get-tuple-element.8), channel_id=5, replica_groups=mesh['gx'=8,'yz'=16] {'yz'}, dimensions={0}, use_global_device_ids=true | all-gather | bytes 278528 | tf_op jit(solution)/shard_map/all_gather | solution.py:45
  568.3 18.6 %all_to_all.316 = bf16[16,8,1024]{2,0,1:T(8,128)(2,1)S(1)} all-to-all(bf16[16,8,1024]{2,0,1:T(8,128)(2,1)S(1)} %copy.84), channel_id=1, replica_groups=mesh['gx'=8,'yz'=16] {'gx'}, dimensions={1} | all-to-all | bytes 524288 | tf_op jit(solution)/shard_map/all_to_all | solution.py:46
  586.9 5.5 fusion.109
  592.4 28.0 %reduce-scatter.21.cloned.1.call-done = f32[16,3584]{1,0:T(8,128)} async-done(((f32[128,3584]{1,0:T(8,128)}), f32[16,3584]{1,0:T(8,128)}) %reduce-scatter.21.cloned.1.call-update) | async-done | bytes 229392 | tf_op jit(solution)/shard_map/reduce_scatter | solution.py:51
  621.9 13.3 %all_to_all.317 = bf16[16,2,1792]{2,1,0:T(2,128)(2,1)S(1)} all-to-all(bf16[16,2,1792]{2,1,0:T(2,128)(2,1)S(1)} %reshape.913), channel_id=1, replica_groups=mesh['gx'=8,'yz'=16] {'yz'}, dimensions={0} | all-to-all | bytes 229376 | tf_op jit(solution)/shard_map/all_to_all | solution.py:57
  635.7 18.4 %all-gather.9 = bf16[16,1,28672]{2,1,0:T(2,128)(2,1)S(1)} all-gather(bf16[1,1,28672]{2,1,0:T(2,128)(2,1)S(1)} %convert_bitcast_fusion), channel_id=1, replica_groups=mesh['gx'=8,'yz'=16] {'yz'}, dimensions={0}, use_global_device_ids=true | all-gather | bytes 974848 | tf_op jit(solution)/shard_map/all_gather | solution.py:45
  654.1 6.5 reduce.25
  660.6 2.2 copy.133
  662.8 13.4 %all-to-all-start.14 = ((bf16[16,8,3584]{2,0,1:T(8,128)(2,1)}), bf16[16,8,3584]{2,0,1:T(8,128)(2,1)S(1)}, u32[]{:S(2)}, u32[]{:S(2)}) async-start(bf16[16,8,3584]{2,0,1:T(8,128)(2,1)} %bitcast.194), calls=%async_computation.21 | async-start | bytes 1835008 | tf_op jit(solution)/shard_map/all_to_all | solution.py:46
  677.2 12.7 %all-to-all-done.14 = bf16[16,8,3584]{2,0,1:T(8,128)(2,1)S(1)} async-done(((bf16[16,8,3584]{2,0,1:T(8,128)(2,1)}), bf16[16,8,3584]{2,0,1:T(8,128)(2,1)S(1)}, u32[]{:S(2)}, u32[]{:S(2)}) %all-to-all-start.14) | async-done | bytes 917536 | tf_op jit(solution)/shard_map/all_to_all | solution.py:46
  689.9 3.4 fusion.110
  693.7 25.7 %reduce-scatter.23.cloned.1.call-done = f32[16,512]{1,0:T(8,128)} async-done(((f32[128,512]{1,0:T(8,128)}), f32[16,512]{1,0:T(8,128)}) %reduce-scatter.23.cloned.1.call-update) | async-done | bytes 32784 | tf_op jit(solution)/shard_map/reduce_scatter | solution.py:51
  721.3 6.8 all-to-all-start.15
  728.8 5.8 all-to-all-done.15
  736.0 16.7 %all-gather.4 = bf16[131072]{0:T(1024)(128)(2,1)S(1)} all-gather(bf16[8192]{0:T(1024)(128)(2,1)S(1)} %get-tuple-element.21), channel_id=6, replica_groups=mesh['gx'=8,'yz'=16] {'yz'}, dimensions={0}, use_global_device_ids=true | all-gather | bytes 278528 | tf_op jit(solution)/shard_map/all_gather | solution.py:45
  753.7 13.0 %all-to-all-start.16 = ((bf16[16,8,1024]{2,0,1:T(8,128)(2,1)}), bf16[16,8,1024]{2,0,1:T(8,128)(2,1)S(1)}, u32[]{:S(2)}, u32[]{:S(2)}) async-start(bf16[16,8,1024]{2,0,1:T(8,128)(2,1)} %copy.89), calls=%async_computation.24 | async-start | bytes 524288 | tf_op jit(solution)/shard_map/all_to_all | solution.py:46
  766.8 17.9 %all-gather.5 = bf16[131072]{0:T(1024)(128)(2,1)S(1)} all-gather(bf16[8192]{0:T(1024)(128)(2,1)S(1)} %get-tuple-element.22), channel_id=7, replica_groups=mesh['gx'=8,'yz'=16] {'yz'}, dimensions={0}, use_global_device_ids=true | all-gather | bytes 278528 | tf_op jit(solution)/shard_map/all_gather | solution.py:45
  785.6 9.7 %all-to-all-start.17 = ((bf16[16,8,1024]{2,0,1:T(8,128)(2,1)}), bf16[16,8,1024]{2,0,1:T(8,128)(2,1)S(1)}, u32[]{:S(2)}, u32[]{:S(2)}) async-start(bf16[16,8,1024]{2,0,1:T(8,128)(2,1)} %copy.90), calls=%async_computation.25 | async-start | bytes 524288 | tf_op jit(solution)/shard_map/all_to_all | solution.py:46
  796.3 5.5 all-to-all-done.17
  803.5 143.1 %all-reduce.5.cloned.1.call-done = (f32[128,512]{1,0:T(8,128)}, f32[128,512]{1,0:T(8,128)}) async-done(((f32[128,512]{1,0:T(8,128)}, f32[128,512]{1,0:T(8,128)}), (f32[128,512]{1,0:T(8,128)}, f32[128,512]{1,0:T(8,128)})) %all-reduce.5.cloned.1.call-update) | async-done | bytes 524304
  947.9 2.1 fusion.82
  953.4 2.0 fusion.85
  (168 shorter events, 54.9 us)
Async XLA Ops:
  7.2 41.5 %copy-start = (bf16[1024,640]{1,0:T(8,128)(2,1)S(1)}, bf16[1024,640]{1,0:T(8,128)(2,1)}, u32[]{:S(2)}) copy-start(bf16[1024,640]{1,0:T(8,128)(2,1)} %param.23) | copy-start | bytes 3932164
  7.2 69.0 %reduce-scatter.9.cloned.1.call-start = ((), (), s32[]{:S(2)}) async-start(), calls=%async_computation.26 | async-start | bytes 368640 | tf_op jit(solution)/shard_map/reduce_scatter | solution.py:51
  78.7 13.2 %all-to-all-start.1 = ((bf16[16,2,320]{2,1,0:T(2,128)(2,1)}), bf16[16,2,320]{2,1,0:T(2,128)(2,1)S(1)}, u32[]{:S(2)}, u32[]{:S(2)}) async-start(bf16[16,2,320]{2,1,0:T(2,128)(2,1)} %reshape.901), calls=%async_computation.2 | async-start | bytes 49152 | tf_op jit(solution)/shard_map/all_to_all | solution.py:57
  85.4 79.2 %reduce-scatter.11.cloned.1.call-start = ((), (), s32[]{:S(2)}) async-start(), calls=%async_computation.27 | async-start | bytes 294912 | tf_op jit(solution)/shard_map/reduce_scatter | solution.py:51
  85.5 8.8 copy-start.15
  85.5 2.4 copy-start.4
  92.0 2.3 copy-start.5
  92.7 0.6 copy-start.11
  92.7 2.2 copy-start.13
  113.7 66.8 %copy-start.3 = (bf16[2,1,8192]{2,0,1:T(2,128)(2,1)S(1)}, bf16[2,1,8192]{2,0,1:T(2,128)(2,1)}, u32[]{:S(2)}) copy-start(bf16[2,1,8192]{2,0,1:T(2,128)(2,1)} %param.15) | copy-start | bytes 98308
  138.9 117.8 %reduce-scatter.13.cloned.1.call-start = ((), (), s32[]{:S(2)}) async-start(), calls=%async_computation.28 | async-start | bytes 2064384 | tf_op jit(solution)/shard_map/reduce_scatter | solution.py:51
  228.7 133.1 %reduce-scatter.15.cloned.1.call-start = ((), (), s32[]{:S(2)}) async-start(), calls=%async_computation.29 | async-start | bytes 294912 | tf_op jit(solution)/shard_map/reduce_scatter | solution.py:51
  308.1 26.6 %copy-start.1 = (bf16[3584,512]{1,0:T(8,128)(2,1)S(1)}, bf16[3584,512]{1,0:T(8,128)(2,1)}, u32[]{:S(2)}) copy-start(bf16[3584,512]{1,0:T(8,128)(2,1)} %param.27) | copy-start | bytes 11010052
  336.1 110.6 %reduce-scatter.17.cloned.1.call-start = ((), (), s32[]{:S(2)}) async-start(), calls=%async_computation.30 | async-start | bytes 368640 | tf_op jit(solution)/shard_map/reduce_scatter | solution.py:51
  379.8 78.6 %copy-start.12 = (bf16[1,8,64]{2,1,0:T(8,128)(2,1)S(1)}, bf16[1,8,64]{2,1,0:T(8,128)(2,1)}, u32[]{:S(2)}) copy-start(bf16[1,8,64]{2,1,0:T(8,128)(2,1)} %copy-done.11) | copy-start | bytes 3076
  379.8 78.6 %copy-start.14 = (bf16[1,8,64]{2,1,0:T(8,128)(2,1)S(1)}, bf16[1,8,64]{2,1,0:T(8,128)(2,1)}, u32[]{:S(2)}) copy-start(bf16[1,8,64]{2,1,0:T(8,128)(2,1)} %copy-done.13) | copy-start | bytes 3076
  398.1 71.4 %copy-start.16 = (pred[1024]{0:T(1024)(128)(4,1)S(1)}, pred[1024]{0:T(1024)(128)(4,1)}, u32[]{:S(2)}) copy-start(pred[1024]{0:T(1024)(128)(4,1)} %copy-done.15) | copy-start | bytes 3076
  421.0 49.7 %copy-start.17 = (bf16[1,1,8,128]{3,1,2,0:T(2,128)(2,1)S(1)}, bf16[1,1,8,128]{3,1,2,0:T(2,128)(2,1)}, u32[]{:S(2)}) copy-start(bf16[1,1,8,128]{3,1,2,0:T(2,128)(2,1)} %get-tuple-element.12) | copy-start | bytes 6148
  451.4 13.4 %all-to-all-start.9 = ((bf16[16,2,320]{2,1,0:T(2,128)(2,1)}), bf16[16,2,320]{2,1,0:T(2,128)(2,1)}, u32[]{:S(2)}, u32[]{:S(2)}) async-start(bf16[16,2,320]{2,1,0:T(2,128)(2,1)} %reshape.909), calls=%async_computation.14 | async-start | bytes 49152 | tf_op jit(solution)/shard_map/all_to_all | solution.py:57
  458.3 77.3 %reduce-scatter.19.cloned.1.call-start = ((), (), s32[]{:S(2)}) async-start(), calls=%async_computation.31 | async-start | bytes 294912 | tf_op jit(solution)/shard_map/reduce_scatter | solution.py:51
  466.3 4.0 copy-start.18
  466.3 4.7 copy-start.6
  470.9 37.9 %copy-start.2 = (bf16[1024,512]{1,0:T(8,128)(2,1)S(1)}, bf16[1024,512]{1,0:T(8,128)(2,1)}, u32[]{:S(2)}) copy-start(bf16[1024,512]{1,0:T(8,128)(2,1)} %param.24) | copy-start | bytes 3145732
  488.5 62.9 %copy-start.8 = (f32[8192]{0:T(1024)S(1)}, f32[8192]{0:T(1024)}, u32[]{:S(2)}) copy-start(f32[8192]{0:T(1024)} %param.25) | copy-start | bytes 98308
  509.8 110.5 %reduce-scatter.21.cloned.1.call-start = ((), (), s32[]{:S(2)}) async-start(), calls=%async_computation.32 | async-start | bytes 2064384 | tf_op jit(solution)/shard_map/reduce_scatter | solution.py:51
  660.6 16.3 %copy-start.19 = (s32[512]{0:T(512)S(1)}, s32[512]{0:T(512)}, u32[]{:S(2)}) copy-start(s32[512]{0:T(512)} %param.20) | copy-start | bytes 6148
  660.6 16.3 %copy-start.20 = (s32[1,16]{1,0:T(1,128)S(1)}, s32[1,16]{1,0:T(1,128)}, u32[]{:S(2)}) copy-start(s32[1,16]{1,0:T(1,128)} %param.19) | copy-start | bytes 196
  662.8 27.0 %all-to-all-start.14 = ((bf16[16,8,3584]{2,0,1:T(8,128)(2,1)}), bf16[16,8,3584]{2,0,1:T(8,128)(2,1)S(1)}, u32[]{:S(2)}, u32[]{:S(2)}) async-start(bf16[16,8,3584]{2,0,1:T(8,128)(2,1)} %bitcast.194), calls=%async_computation.21 | async-start | bytes 1835008 | tf_op jit(solution)/shard_map/all_to_all | solution.py:46
  676.3 43.1 %reduce-scatter.23.cloned.1.call-start = ((), (), s32[]{:S(2)}) async-start(), calls=%async_computation.33 | async-start | bytes 294912 | tf_op jit(solution)/shard_map/reduce_scatter | solution.py:51
  689.9 46.1 %copy-start.9 = (bf16[8192]{0:T(1024)(128)(2,1)S(1)}, bf16[8192]{0:T(1024)(128)(2,1)}, u32[]{:S(2)}) copy-start(bf16[8192]{0:T(1024)(128)(2,1)} %get-tuple-element.11) | copy-start | bytes 49156
  689.9 46.1 %copy-start.10 = (f32[8192]{0:T(1024)S(1)}, f32[8192]{0:T(1024)}, u32[]{:S(2)}) copy-start(f32[8192]{0:T(1024)} %param.28) | copy-start | bytes 98308
  721.3 13.2 %all-to-all-start.15 = ((bf16[16,2,256]{2,1,0:T(2,128)(2,1)}), bf16[16,2,256]{2,1,0:T(2,128)(2,1)S(1)}, u32[]{:S(2)}, u32[]{:S(2)}) async-start(bf16[16,2,256]{2,1,0:T(2,128)(2,1)} %reshape.915), calls=%async_computation.23 | async-start | bytes 32768 | tf_op jit(solution)/shard_map/all_to_all | solution.py:57
  735.3 60.1 %copy-start.7 = (bf16[64,512]{1,0:T(8,128)(2,1)S(1)}, bf16[64,512]{1,0:T(8,128)(2,1)}, u32[]{:S(2)}) copy-start(bf16[64,512]{1,0:T(8,128)(2,1)} %param.29) | copy-start | bytes 196612
  753.7 32.0 %all-to-all-start.16 = ((bf16[16,8,1024]{2,0,1:T(8,128)(2,1)}), bf16[16,8,1024]{2,0,1:T(8,128)(2,1)S(1)}, u32[]{:S(2)}, u32[]{:S(2)}) async-start(bf16[16,8,1024]{2,0,1:T(8,128)(2,1)} %copy.89), calls=%async_computation.24 | async-start | bytes 524288 | tf_op jit(solution)/shard_map/all_to_all | solution.py:46
  785.6 16.2 %all-to-all-start.17 = ((bf16[16,8,1024]{2,0,1:T(8,128)(2,1)}), bf16[16,8,1024]{2,0,1:T(8,128)(2,1)S(1)}, u32[]{:S(2)}, u32[]{:S(2)}) async-start(bf16[16,8,1024]{2,0,1:T(8,128)(2,1)} %copy.90), calls=%async_computation.25 | async-start | bytes 524288 | tf_op jit(solution)/shard_map/all_to_all | solution.py:46
  795.4 151.2 %all-reduce.5.cloned.1.call-start = ((), (), s32[]{:S(2)}) async-start(), calls=%async_computation.34 | async-start | bytes 1048576
Sparse Core Ops, SparseCore 0:
  49.9 26.2 reduce-scatter.8
  139.0 25.6 reduce-scatter.10
  228.8 27.7 reduce-scatter.12
  336.2 25.5 reduce-scatter.14
  421.1 25.5 reduce-scatter.16
  510.0 25.6 reduce-scatter.18
  592.5 27.7 reduce-scatter.20
  693.4 25.8 reduce-scatter.22
  802.9 143.5 all-reduce.4
where the time goes:
time: 968 us; the launch traced here: 965 us
  blocking collectives  386 us (40%)
  waiting for transfers between devices  384 us (40%)
  other arithmetic  61.6 us (6%)
  starting transfers between devices  56.9 us (6%)
  local copies, waits for them, and re-layouts  27.6 us (3%)
  matrix products  27 us (3%)
  between operations  21.2 us (2%)
    reduce_scatter x8, waiting for transfers between devices, project(): lax.psum_scatter(jnp.dot(spread, weight, preferred_element_type=jnp.float...  209 us
    all_gather x10, blocking collectives, spread_rows(): gathered = lax.all_gather(inputs, 'yz', axis=0, tiled=True)  185 us
    unnamed x10, waiting for transfers between devices  143 us
    all_to_all x7, blocking collectives, spread_rows(): lax.all_to_all(gathered, 'gx', split_axis=1, concat_axis=0, tiled=True)  135 us
    all_to_all x5, blocking collectives, project(): lax.all_to_all(summed.astype(jnp.bfloat16), 'yz', split_axis=0, concat_ax...  66.1 us
    all_to_all x3, starting transfers between devices, spread_rows(): lax.all_to_all(gathered, 'gx', split_axis=1, concat_axis=0, tiled=True)  36.2 us
    dot_general x8, matrix products, project(): jnp.dot(spread, weight, preferred_element_type=jnp.float32)  21.2 us
    all_to_all x3, starting transfers between devices, project(): lax.all_to_all(summed.astype(jnp.bfloat16), 'yz', split_axis=0, concat_ax...  20.4 us
  transfers between devices with their start and end apart: 15, of which 14 were waited for; matrix products, arithmetic and copies ran while one was open for 1% of the time, Pallas kernels for 0%

commit v1 on v0

--- a/solution.py
+++ b/solution.py
@@ -12,6 +12,27 @@
 ELEMENTS = 16
 NORM_EPS = 1e-05
 ROPE_THETA = 500000.0
+
+
+def gather_around(x, axis, dim):
+    peers, mine, span = (lax.axis_size(axis), lax.axis_index(axis), x.shape[dim])
+    right = [(i, (i + 1) % peers) for i in range(peers)]
+    left = [(i, (i - 1) % peers) for i in range(peers)]
+    out = jnp.zeros((*x.shape[:dim], peers * span, *x.shape[dim + 1 :]), x.dtype)
+    out = lax.dynamic_update_slice_in_dim(out, x, mine * span, axis=dim)
+    from_left = from_right = x
+    half = peers // 2
+    for step in range(1, half + 1):
+        from_left = lax.ppermute(from_left, axis, right)
+        out = lax.dynamic_update_slice_in_dim(
+            out, from_left, (mine - step) % peers * span, axis=dim
+        )
+        if step < peers - half:
+            from_right = lax.ppermute(from_right, axis, left)
+            out = lax.dynamic_update_slice_in_dim(
+                out, from_right, (mine + step) % peers * span, axis=dim
+            )
+    return out
 
 
 def norm_rows(values, gain_vec):
@@ -42,7 +63,7 @@
 
 
 def spread_rows(inputs):
-    gathered = lax.all_gather(inputs, "yz", axis=0, tiled=True)
+    gathered = gather_around(inputs, "yz", 0)
     return lax.all_to_all(gathered, "gx", split_axis=1, concat_axis=0, tiled=True)
 
 

time: 968 us -> 1440 us (1.49)
  starting transfers between devices: 56.9 us -> 352 us
  local copies, waits for them, and re-layouts: 27.6 us -> 252 us
  blocking collectives: 386 us -> 248 us
  waiting for transfers between devices: 384 us -> 481 us
  other arithmetic: 61.6 us -> 44 us
    ppermute x0 -> x150, starting transfers between devices: none -> 310 us  [the longest x70 297 us: gather_around(): from_right = lax.ppermute(from_right, axis, left)]
    dynamic_update_slice x0 -> x160, local copies, waits for them, and re-layouts: none -> 213 us  [the longest x80 107 us: gather_around(): lax.dynamic_update_slice_in_dim(out, from_left, (mine - step) % peers * s...]
    all_gather x10 -> x0, blocking collectives: 185 us -> none  [spread_rows(): gathered = lax.all_gather(inputs, 'yz', axis=0, tiled=True)]
    ppermute x0 -> x150, waiting for transfers between devices: none -> 88.3 us  [the longest x80 88 us: gather_around(): from_left = lax.ppermute(from_left, axis, right)]
    all_to_all x7 -> x8, blocking collectives: 135 us -> 182 us  [spread_rows(): lax.all_to_all(gathered, 'gx', split_axis=1, concat_axis=0, tiled=True)]
    all_gather x4 -> x0, other arithmetic: 19.1 us -> none  [spread_rows(): gathered = lax.all_gather(inputs, 'yz', axis=0, tiled=True)]
    reduce_scatter x8, waiting for transfers between devices: 209 us -> 227 us  [project(): lax.psum_scatter(jnp.dot(spread, weight, preferred_element_type=jnp.float...]
    all_to_all x3 -> x2, starting transfers between devices: 36.2 us -> 21 us  [spread_rows(): lax.all_to_all(gathered, 'gx', split_axis=1, concat_axis=0, tiled=True)]
  transfers between devices with their start and end apart: 15 -> 164, of which waited for: 14 -> 73; matrix products, arithmetic and copies ran while one was open for 1% -> 15% of each run, Pallas kernels for 0% -> 0%
where the time goes in v1:
time: 1440 us; the launch traced here: 1430 us
  waiting for transfers between devices  481 us (33%)
  starting transfers between devices  352 us (24%)
  local copies, waits for them, and re-layouts  252 us (18%)
  blocking collectives  248 us (17%)
  other arithmetic  44 us (3%)
  matrix products  25 us (2%)
  between operations  23.2 us (2%)
    ppermute x70, starting transfers between devices, gather_around(): from_right = lax.ppermute(from_right, axis, left)  297 us
    reduce_scatter x8, waiting for transfers between devices, project(): lax.psum_scatter(jnp.dot(spread, weight, preferred_element_type=jnp.float...  227 us
    all_to_all x8, blocking collectives, spread_rows(): lax.all_to_all(gathered, 'gx', split_axis=1, concat_axis=0, tiled=True)  182 us
    unnamed x10, waiting for transfers between devices  146 us
    dynamic_update_slice x80, local copies, waits for them, and re-layouts, gather_around(): lax.dynamic_update_slice_in_dim(out, from_left, (mine - step) % peers * s...  107 us
    dynamic_update_slice x70, local copies, waits for them, and re-layouts, gather_around(): lax.dynamic_update_slice_in_dim(out, from_right, (mine + step) % peers *...  93.6 us
    ppermute x80, waiting for transfers between devices, gather_around(): from_left = lax.ppermute(from_left, axis, right)  88 us
    all_to_all x5, blocking collectives, project(): lax.all_to_all(summed.astype(jnp.bfloat16), 'yz', split_axis=0, concat_ax...  66.1 us
  transfers between devices with their start and end apart: 164, of which 73 were waited for; matrix products, arithmetic and copies ran while one was open for 15% of the time, Pallas kernels for 0%

profile of v1, /device:TPU:1, one launch (start us, length us, event | category | flops | bytes accessed | tf_op | source)
XLA Modules:
  0.0 1425.6 jit_solution(6444133985962528771)
XLA Ops:
  13.3 5.0 collective-permute-start.1
  19.5 4.9 collective-permute-start.3
  25.6 4.9 collective-permute-start.5
  31.6 4.9 collective-permute-start.7
  37.7 4.9 collective-permute-start.9
  43.8 4.9 collective-permute-start.11
  49.9 4.9 collective-permute-start.13
  63.9 19.0 %all_to_all.306 = bf16[16,8,1024]{2,0,1:T(8,128)(2,1)S(1)} all-to-all(bf16[16,8,1024]{2,0,1:T(8,128)(2,1)S(1)} %bitcast.236), channel_id=1, replica_groups=mesh['gx'=8,'yz'=16] {'gx'}, dimensions={1} | all-to-all | bytes 524288 | tf_op jit(solution)/shard_map/all_to_all | solution.py:67
  84.7 27.5 %reduce-scatter.9.cloned.1.call-done = f32[16,640]{1,0:T(8,128)} async-done(((f32[128,640]{1,0:T(8,128)}), f32[16,640]{1,0:T(8,128)}) %reduce-scatter.9.cloned.1.call-update) | async-done | bytes 40976 | tf_op jit(solution)/shard_map/reduce_scatter | solution.py:72
  114.7 6.8 all-to-all-start.1
  139.6 4.8 collective-permute-start.18
  205.6 21.1 %all_to_all.307 = bf16[16,8,1024]{2,0,1:T(8,128)(2,1)S(1)} all-to-all(bf16[16,8,1024]{2,0,1:T(8,128)(2,1)S(1)} %bitcast.238), channel_id=1, replica_groups=mesh['gx'=8,'yz'=16] {'gx'}, dimensions={1} | all-to-all | bytes 524288 | tf_op jit(solution)/shard_map/all_to_all | solution.py:67
  229.1 28.1 %reduce-scatter.11.cloned.1.call-done = f32[16,512]{1,0:T(8,128)} async-done(((f32[128,512]{1,0:T(8,128)}), f32[16,512]{1,0:T(8,128)}) %reduce-scatter.11.cloned.1.call-update) | async-done | bytes 32784 | tf_op jit(solution)/shard_map/reduce_scatter | solution.py:72
  258.5 13.0 all_to_all.308
  348.2 21.1 %all_to_all.309 = bf16[16,8,1024]{2,0,1:T(8,128)(2,1)S(1)} all-to-all(bf16[16,8,1024]{2,0,1:T(8,128)(2,1)S(1)} %bitcast.240), channel_id=1, replica_groups=mesh['gx'=8,'yz'=16] {'gx'}, dimensions={1} | all-to-all | bytes 524288 | tf_op jit(solution)/shard_map/all_to_all | solution.py:67
  369.3 5.5 fusion.107
  374.9 30.3 %reduce-scatter.13.cloned.1.call-done = f32[16,3584]{1,0:T(8,128)} async-done(((f32[128,3584]{1,0:T(8,128)}), f32[16,3584]{1,0:T(8,128)}) %reduce-scatter.13.cloned.1.call-update) | async-done | bytes 229392 | tf_op jit(solution)/shard_map/reduce_scatter | solution.py:72
  410.5 13.7 all_to_all.310
  534.3 28.6 %all_to_all.311 = bf16[16,8,3584]{2,0,1:T(8,128)(2,1)S(1)} all-to-all(bf16[16,8,3584]{2,0,1:T(8,128)(2,1)S(1)} %bitcast.225), channel_id=1, replica_groups=mesh['gx'=8,'yz'=16] {'gx'}, dimensions={1} | all-to-all | bytes 1835008 | tf_op jit(solution)/shard_map/all_to_all | solution.py:67
  564.3 27.8 %reduce-scatter.15.cloned.1.call-done = f32[16,512]{1,0:T(8,128)} async-done(((f32[128,512]{1,0:T(8,128)}), f32[16,512]{1,0:T(8,128)}) %reduce-scatter.15.cloned.1.call-update) | async-done | bytes 32784 | tf_op jit(solution)/shard_map/reduce_scatter | solution.py:72
  593.5 13.0 all_to_all.312
  682.6 21.2 %all_to_all.313 = bf16[16,8,1024]{2,0,1:T(8,128)(2,1)S(1)} all-to-all(bf16[16,8,1024]{2,0,1:T(8,128)(2,1)S(1)} %bitcast.242), channel_id=1, replica_groups=mesh['gx'=8,'yz'=16] {'gx'}, dimensions={1} | all-to-all | bytes 524288 | tf_op jit(solution)/shard_map/all_to_all | solution.py:67
  705.5 27.5 %reduce-scatter.17.cloned.1.call-done = f32[16,640]{1,0:T(8,128)} async-done(((f32[128,640]{1,0:T(8,128)}), f32[16,640]{1,0:T(8,128)}) %reduce-scatter.17.cloned.1.call-update) | async-done | bytes 40976 | tf_op jit(solution)/shard_map/reduce_scatter | solution.py:72
  737.7 6.9 all-to-all-start.9
  745.4 5.8 all-to-all-done.9
  764.0 4.8 collective-permute-start.78
  770.1 4.8 collective-permute-start.80
  776.7 4.8 collective-permute-start.82
  782.8 4.8 collective-permute-start.84
  788.9 4.8 collective-permute-start.86
  795.0 4.8 collective-permute-start.88
  809.3 21.1 %all_to_all.314 = bf16[16,8,1024]{2,0,1:T(8,128)(2,1)S(1)} all-to-all(bf16[16,8,1024]{2,0,1:T(8,128)(2,1)S(1)} %bitcast.244), channel_id=1, replica_groups=mesh['gx'=8,'yz'=16] {'gx'}, dimensions={1} | all-to-all | bytes 524288 | tf_op jit(solution)/shard_map/all_to_all | solution.py:67
  831.6 28.1 %reduce-scatter.19.cloned.1.call-done = f32[16,512]{1,0:T(8,128)} async-done(((f32[128,512]{1,0:T(8,128)}), f32[16,512]{1,0:T(8,128)}) %reduce-scatter.19.cloned.1.call-update) | async-done | bytes 32784 | tf_op jit(solution)/shard_map/reduce_scatter | solution.py:72
  860.9 13.0 all_to_all.315
  881.6 4.8 collective-permute-start.93
  887.7 4.8 collective-permute-start.95
  894.4 4.8 collective-permute-start.97
  900.5 4.8 collective-permute-start.99
  906.6 4.8 collective-permute-start.101
  912.7 4.8 collective-permute-start.103
  926.6 21.1 %all_to_all.316 = bf16[16,8,1024]{2,0,1:T(8,128)(2,1)S(1)} all-to-all(bf16[16,8,1024]{2,0,1:T(8,128)(2,1)S(1)} %bitcast.246), channel_id=1, replica_groups=mesh['gx'=8,'yz'=16] {'gx'}, dimensions={1} | all-to-all | bytes 524288 | tf_op jit(solution)/shard_map/all_to_all | solution.py:67
  947.7 5.5 fusion.111
  953.2 30.3 %reduce-scatter.21.cloned.1.call-done = f32[16,3584]{1,0:T(8,128)} async-done(((f32[128,3584]{1,0:T(8,128)}), f32[16,3584]{1,0:T(8,128)}) %reduce-scatter.21.cloned.1.call-update) | async-done | bytes 229392 | tf_op jit(solution)/shard_map/reduce_scatter | solution.py:72
  985.1 13.4 all_to_all.317
  1005.9 5.0 collective-permute-start.108
  1012.8 5.0 collective-permute-start.110
  1020.6 5.3 collective-permute-start.112
  1028.4 5.2 collective-permute-start.114
  1035.4 5.2 collective-permute-start.116
  1042.3 5.3 collective-permute-start.118
  1089.4 29.0 %all_to_all.318 = bf16[16,8,3584]{2,0,1:T(8,128)(2,1)S(1)} all-to-all(bf16[16,8,3584]{2,0,1:T(8,128)(2,1)S(1)} %bitcast.227), channel_id=1, replica_groups=mesh['gx'=8,'yz'=16] {'gx'}, dimensions={1} | all-to-all | bytes 1835008 | tf_op jit(solution)/shard_map/all_to_all | solution.py:67
  1119.8 27.9 %reduce-scatter.23.cloned.1.call-done = f32[16,512]{1,0:T(8,128)} async-done(((f32[128,512]{1,0:T(8,128)}), f32[16,512]{1,0:T(8,128)}) %reduce-scatter.23.cloned.1.call-update) | async-done | bytes 32784 | tf_op jit(solution)/shard_map/reduce_scatter | solution.py:72
  1149.6 6.8 all-to-all-start.15
  1157.1 5.8 all-to-all-done.15
  1170.5 4.8 collective-permute-start.136
  1177.5 4.8 collective-permute-start.138
  1183.8 5.2 collective-permute-start.140
  1197.5 4.8 collective-permute-start.144
  1203.8 4.8 collective-permute-start.146
  1216.7 4.8 collective-permute-start.148
  1223.7 16.2 %all-to-all-start.16 = ((bf16[16,8,1024]{2,0,1:T(8,128)(2,1)}), bf16[16,8,1024]{2,0,1:T(8,128)(2,1)S(1)}, u32[]{:S(2)}, u32[]{:S(2)}) async-start(bf16[16,8,1024]{2,0,1:T(8,128)(2,1)} %bitcast.211), calls=%async_computation.24 | async-start | bytes 524288 | tf_op jit(solution)/shard_map/all_to_all | solution.py:67
  1248.5 4.8 all-to-all-start.17
  1254.3 5.5 all-to-all-done.17
  1261.4 145.7 %all-reduce.5.cloned.1.call-done = (f32[128,512]{1,0:T(8,128)}, f32[128,512]{1,0:T(8,128)}) async-done(((f32[128,512]{1,0:T(8,128)}, f32[128,512]{1,0:T(8,128)}), (f32[128,512]{1,0:T(8,128)}, f32[128,512]{1,0:T(8,128)})) %all-reduce.5.cloned.1.call-update) | async-done | bytes 524304
  (725 shorter events, 555.2 us)
Async XLA Ops:
  7.2 105.0 %reduce-scatter.9.cloned.1.call-start = ((), (), s32[]{:S(2)}) async-start(), calls=%async_computation.26 | async-start | bytes 368640 | tf_op jit(solution)/shard_map/reduce_scatter | solution.py:72
  11.1 8.4 collective-permute-start
  49.9 13.0 collective-permute-start.13
  56.0 7.4 collective-permute-start.14
  114.7 13.2 all-to-all-start.1
  121.5 135.6 %reduce-scatter.11.cloned.1.call-start = ((), (), s32[]{:S(2)}) async-start(), calls=%async_computation.27 | async-start | bytes 294912 | tf_op jit(solution)/shard_map/reduce_scatter | solution.py:72
  171.2 30.1 %collective-permute-start.28 = (bf16[1,8192]{1,0:T(2,128)(2,1)}, bf16[1,8192]{1,0:T(2,128)(2,1)}, u32[]{:S(2)}, u32[]{:S(2)}) collective-permute-start(bf16[1,8192]{1,0:T(2,128)(2,1)} %collective-permute-done.26), channel_id=1, source_target_pairs={{0,15},{1,0},{2,1},{3,2},{4,3},{5,4},{6,5},{7,6},{8,7},{9,8},{10,9... | collective-permute-start | bytes 49160 | tf_op jit(solution)/shard_map/ppermute | solution.py:31
  176.8 26.2 %collective-permute-start.29 = (bf16[1,8192]{1,0:T(2,128)(2,1)}, bf16[1,8192]{1,0:T(2,128)(2,1)}, u32[]{:S(2)}, u32[]{:S(2)}) collective-permute-start(bf16[1,8192]{1,0:T(2,128)(2,1)} %collective-permute-done.27), channel_id=1, source_target_pairs={{0,1},{1,2},{2,3},{3,4},{4,5},{5,6},{6,7},{7,8},{8,9},{9,10},{10,1... | collective-permute-start | bytes 49160 | tf_op jit(solution)/shard_map/ppermute | solution.py:26
  229.1 176.1 %reduce-scatter.13.cloned.1.call-start = ((), (), s32[]{:S(2)}) async-start(), calls=%async_computation.28 | async-start | bytes 2064384 | tf_op jit(solution)/shard_map/reduce_scatter | solution.py:72
  313.8 30.0 %collective-permute-start.43 = (bf16[1,8192]{1,0:T(2,128)(2,1)}, bf16[1,8192]{1,0:T(2,128)(2,1)}, u32[]{:S(2)}, u32[]{:S(2)}) collective-permute-start(bf16[1,8192]{1,0:T(2,128)(2,1)} %collective-permute-done.41), channel_id=1, source_target_pairs={{0,15},{1,0},{2,1},{3,2},{4,3},{5,4},{6,5},{7,6},{8,7},{9,8},{10,9... | collective-permute-start | bytes 49160 | tf_op jit(solution)/shard_map/ppermute | solution.py:31
  319.4 26.1 %collective-permute-start.44 = (bf16[1,8192]{1,0:T(2,128)(2,1)}, bf16[1,8192]{1,0:T(2,128)(2,1)}, u32[]{:S(2)}, u32[]{:S(2)}) collective-permute-start(bf16[1,8192]{1,0:T(2,128)(2,1)} %collective-permute-done.42), channel_id=1, source_target_pairs={{0,1},{1,2},{2,3},{3,4},{4,5},{5,6},{6,7},{7,8},{8,9},{9,10},{10,1... | collective-permute-start | bytes 49160 | tf_op jit(solution)/shard_map/ppermute | solution.py:26
  374.8 217.3 %reduce-scatter.15.cloned.1.call-start = ((), (), s32[]{:S(2)}) async-start(), calls=%async_computation.29 | async-start | bytes 294912 | tf_op jit(solution)/shard_map/reduce_scatter | solution.py:72
  427.1 7.0 collective-permute-start.45
  434.1 7.0 collective-permute-start.47
  441.1 7.6 collective-permute-start.49
  441.7 6.9 collective-permute-start.50
  448.7 8.0 collective-permute-start.51
  449.3 7.3 collective-permute-start.52
  456.6 7.0 collective-permute-start.53
  463.6 7.0 collective-permute-start.55
  470.6 7.1 collective-permute-start.57
  471.2 54.9 %collective-permute-start.58 = (bf16[1,28672]{1,0:T(2,128)(2,1)}, bf16[1,28672]{1,0:T(2,128)(2,1)}, u32[]{:S(2)}, u32[]{:S(2)}) collective-permute-start(bf16[1,28672]{1,0:T(2,128)(2,1)} %collective-permute-done.56), channel_id=1, source_target_pairs={{0,15},{1,0},{2,1},{3,2},{4,3},{5,4},{6,5},{7,6},{8,7},{9,8},{10,9... | collective-permute-start | bytes 172040 | tf_op jit(solution)/shard_map/ppermute | solution.py:31
  477.6 51.9 %collective-permute-start.59 = (bf16[1,28672]{1,0:T(2,128)(2,1)}, bf16[1,28672]{1,0:T(2,128)(2,1)}, u32[]{:S(2)}, u32[]{:S(2)}) collective-permute-start(bf16[1,28672]{1,0:T(2,128)(2,1)} %collective-permute-done.57), channel_id=1, source_target_pairs={{0,1},{1,2},{2,3},{3,4},{4,5},{5,6},{6,7},{7,8},{8,9},{9,10},{10,1... | collective-permute-start | bytes 172040 | tf_op jit(solution)/shard_map/ppermute | solution.py:26
  564.3 168.7 %reduce-scatter.17.cloned.1.call-start = ((), (), s32[]{:S(2)}) async-start(), calls=%async_computation.30 | async-start | bytes 368640 | tf_op jit(solution)/shard_map/reduce_scatter | solution.py:72
  648.0 30.2 %collective-permute-start.73 = (bf16[1,8192]{1,0:T(2,128)(2,1)}, bf16[1,8192]{1,0:T(2,128)(2,1)}, u32[]{:S(2)}, u32[]{:S(2)}) collective-permute-start(bf16[1,8192]{1,0:T(2,128)(2,1)} %collective-permute-done.71), channel_id=1, source_target_pairs={{0,15},{1,0},{2,1},{3,2},{4,3},{5,4},{6,5},{7,6},{8,7},{9,8},{10,9... | collective-permute-start | bytes 49160 | tf_op jit(solution)/shard_map/ppermute | solution.py:31
  653.6 26.3 %collective-permute-start.74 = (bf16[1,8192]{1,0:T(2,128)(2,1)}, bf16[1,8192]{1,0:T(2,128)(2,1)}, u32[]{:S(2)}, u32[]{:S(2)}) collective-permute-start(bf16[1,8192]{1,0:T(2,128)(2,1)} %collective-permute-done.72), channel_id=1, source_target_pairs={{0,1},{1,2},{2,3},{3,4},{4,5},{5,6},{6,7},{7,8},{8,9},{9,10},{10,1... | collective-permute-start | bytes 49160 | tf_op jit(solution)/shard_map/ppermute | solution.py:26
  737.7 13.5 all-to-all-start.9
  744.6 115.0 %reduce-scatter.19.cloned.1.call-start = ((), (), s32[]{:S(2)}) async-start(), calls=%async_computation.31 | async-start | bytes 294912 | tf_op jit(solution)/shard_map/reduce_scatter | solution.py:72
  795.0 13.3 collective-permute-start.88
  801.1 7.7 collective-permute-start.89
  831.5 152.0 %reduce-scatter.21.cloned.1.call-start = ((), (), s32[]{:S(2)}) async-start(), calls=%async_computation.32 | async-start | bytes 2064384 | tf_op jit(solution)/shard_map/reduce_scatter | solution.py:72
  912.7 12.9 collective-permute-start.103
  918.8 7.3 collective-permute-start.104
  953.2 194.5 %reduce-scatter.23.cloned.1.call-start = ((), (), s32[]{:S(2)}) async-start(), calls=%async_computation.33 | async-start | bytes 294912 | tf_op jit(solution)/shard_map/reduce_scatter | solution.py:72
  998.8 7.0 collective-permute-start.105
  1005.9 7.0 collective-permute-start.107
  1005.9 7.0 collective-permute-start.108
  1012.8 7.7 collective-permute-start.109
  1012.8 7.8 collective-permute-start.110
  1020.6 7.8 collective-permute-start.111
  1020.6 7.7 collective-permute-start.112
  1028.4 7.0 collective-permute-start.113
  1028.4 7.0 collective-permute-start.114
  1035.3 7.0 collective-permute-start.115
  1035.4 7.0 collective-permute-start.116
  1042.3 7.1 collective-permute-start.117
  1042.3 41.0 %collective-permute-start.118 = (bf16[1,28672]{1,0:T(2,128)(2,1)}, bf16[1,28672]{1,0:T(2,128)(2,1)}, u32[]{:S(2)}, u32[]{:S(2)}) collective-permute-start(bf16[1,28672]{1,0:T(2,128)(2,1)} %collective-permute-done.116), channel_id=1, source_target_pairs={{0,15},{1,0},{2,1},{3,2},{4,3},{5,4},{6,5},{7,6},{8,7},{9,8},{10,9... | collective-permute-start | bytes 172040 | tf_op jit(solution)/shard_map/ppermute | solution.py:31
  1049.4 36.9 %collective-permute-start.119 = (bf16[1,28672]{1,0:T(2,128)(2,1)}, bf16[1,28672]{1,0:T(2,128)(2,1)}, u32[]{:S(2)}, u32[]{:S(2)}) collective-permute-start(bf16[1,28672]{1,0:T(2,128)(2,1)} %collective-permute-done.117), channel_id=1, source_target_pairs={{0,1},{1,2},{2,3},{3,4},{4,5},{5,6},{6,7},{7,8},{8,9},{9,10},{10,1... | collective-permute-start | bytes 172040 | tf_op jit(solution)/shard_map/ppermute | solution.py:26
  1149.6 13.2 all-to-all-start.15
  1164.7 10.6 collective-permute-start.121
  1170.5 7.0 collective-permute-start.136
  1175.3 7.0 collective-permute-start.123
  1175.9 7.0 collective-permute-start.137
  1176.8 7.0 collective-permute-start.124
  1183.8 7.1 collective-permute-start.140
  1203.8 12.9 collective-permute-start.146
  1208.6 13.5 collective-permute-start.133
  1208.8 13.2 collective-permute-start.147
  1210.0 12.5 collective-permute-start.134
  1216.7 30.1 %collective-permute-start.148 = (bf16[1,8192]{1,0:T(2,128)(2,1)S(1)}, bf16[1,8192]{1,0:T(2,128)(2,1)S(1)}, u32[]{:S(2)}, u32[]{:S(2)}) collective-permute-start(bf16[1,8192]{1,0:T(2,128)(2,1)S(1)} %collective-permute-done.146), channel_id=1, source_target_pairs={{0,15},{1,0},{2,1},{3,2},{4,3},{5,4},{6,5},{7,6},{8,7},{9,8},{10,9... | collective-permute-start | bytes 49160 | tf_op jit(solution)/shard_map/ppermute | solution.py:31
  1221.9 25.4 %collective-permute-start.149 = (bf16[1,8192]{1,0:T(2,128)(2,1)S(1)}, bf16[1,8192]{1,0:T(2,128)(2,1)S(1)}, u32[]{:S(2)}, u32[]{:S(2)}) collective-permute-start(bf16[1,8192]{1,0:T(2,128)(2,1)S(1)} %collective-permute-done.147), channel_id=1, source_target_pairs={{0,1},{1,2},{2,3},{3,4},{4,5},{5,6},{6,7},{7,8},{8,9},{9,10},{10,1... | collective-permute-start | bytes 49160 | tf_op jit(solution)/shard_map/ppermute | solution.py:26
  1223.7 24.8 %all-to-all-start.16 = ((bf16[16,8,1024]{2,0,1:T(8,128)(2,1)}), bf16[16,8,1024]{2,0,1:T(8,128)(2,1)S(1)}, u32[]{:S(2)}, u32[]{:S(2)}) async-start(bf16[16,8,1024]{2,0,1:T(8,128)(2,1)} %bitcast.211), calls=%async_computation.24 | async-start | bytes 524288 | tf_op jit(solution)/shard_map/all_to_all | solution.py:67
  1248.5 11.3 all-to-all-start.17
  1253.3 153.8 %all-reduce.5.cloned.1.call-start = ((), (), s32[]{:S(2)}) async-start(), calls=%async_computation.34 | async-start | bytes 1048576
  (172 other events, 1827.4 us)
Sparse Core Ops, SparseCore 0:
  84.2 28.0 reduce-scatter.8
  229.2 27.9 reduce-scatter.10
  375.0 30.1 reduce-scatter.12
  564.4 27.7 reduce-scatter.14
  705.0 27.9 reduce-scatter.16
  831.6 27.9 reduce-scatter.18
  953.3 30.1 reduce-scatter.20
  1119.9 27.7 reduce-scatter.22
  1260.9 146.1 all-reduce.4
